TPU v7x, 128 devices: a whole 4x4x4 slice. The times are simulated.
128 devices in a mesh: grp: 8 (over x, core), blk: 16 (over y, z).
Axes of the slice: x: 4, y: 4, z: 4, core: 2. Of those that a mesh axis runs over, the one named last changes fastest.
Arguments:
- features: bfloat16 [8, 16, 4096, 256], P('grp', 'blk'), may hold values from -6 to 6
- hub_rows: int32 [8, 16, 32], P('grp', 'blk'), may hold values from 0 to 4095
- hub_adjacency: bfloat16 [8, 16, 4096, 512], P('grp', 'blk'), as said below
- tile_row: int32 [8, 16, 160], P('grp', 'blk'), may hold values from 0 to 31
- tile_col: int32 [8, 16, 160], P('grp', 'blk'), may hold values from 0 to 63
- tile_count: int32 [8, 16], P('grp', 'blk'), may hold values from 26 to 160, as said below
- tile_values: bfloat16 [8, 16, 160, 128, 128], P('grp', 'blk'), may hold values from 0 to 0.049804688
- send_rows: int32 [8, 16, 8, 16, 32], P('grp', 'blk'), may hold values from 0 to 4095
- weight: bfloat16 [256, 256], replicated, may hold values from -0.375 to 0.375
Outputs:
- activations: bfloat16 [8, 16, 4096, 256], P('grp', 'blk')
Inputs may be any that keep to these rules, and one draw needn't show every extreme that they name: `tile_count`: some device has exactly 160 live tile slots in every draw. `hub_adjacency`: Non-negative edge weights.
All inputs are finite; a program needn't handle non-finite values.
Results may differ from a plain program's by a relative error of at most 0.0014.
The roundings to bfloat16 on the way count: a program that leaves them out, or rounds other values in their place, can miss the bound.
Values may be sent and summed in bfloat16 or wider, within the bound.
No kernel may reach another device: no remote copies, remote signals or barrier semaphores. Data moves between devices by JAX's collectives and lax.ppermute only.
A program may use at most 128 MiB of HBM per device.

v0:
```python
import jax
import jax.numpy as jnp
from jax import lax
from jax.sharding import PartitionSpec as P

TB = 128


def per_device(
    features,
    hub_rows,
    hub_adjacency,
    tile_row,
    tile_col,
    tile_count,
    tile_values,
    send_rows,
    weight,
):
    local = features[0, 0]
    rows = local.shape[0]
    width = local.shape[1]
    adjacency = hub_adjacency[0, 0]
    hub_block = local[hub_rows[0, 0]]
    hub_part = jnp.dot(
        adjacency,
        lax.all_gather(hub_block, "blk", axis=0, tiled=True),
        preferred_element_type=jnp.float32,
    )
    listing = send_rows[0, 0]
    outgoing = local[listing.reshape(-1)]
    incoming = lax.all_to_all(outgoing, ("grp", "blk"), split_axis=0, concat_axis=0, tiled=True)
    table = jnp.concatenate([local, incoming], 0)
    table_blocks = table.shape[0] // TB
    flat_table = table.reshape(table_blocks, TB * width)
    slots = tile_col.shape[-1]
    selector = (
        tile_col[0, 0][:, None] == jnp.arange(table_blocks, dtype=jnp.int32)[None, :]
    ).astype(jnp.bfloat16)
    picked = jnp.dot(selector, flat_table, preferred_element_type=jnp.float32).astype(jnp.bfloat16)
    picked = picked.reshape(slots, TB, width)
    products = jnp.einsum(
        "tij,tjf->tif", tile_values[0, 0], picked, preferred_element_type=jnp.float32
    )
    row_blocks = rows // TB
    valid = jnp.arange(slots, dtype=jnp.int32) < tile_count[0, 0]
    placing = (
        (jnp.arange(row_blocks, dtype=jnp.int32)[:, None] == tile_row[0, 0][None, :])
        & valid[None, :]
    ).astype(jnp.float32)
    tile_part = jnp.dot(
        placing,
        products.reshape(slots, TB * width),
        precision=lax.Precision.HIGHEST,
        preferred_element_type=jnp.float32,
    )
    aggregated = (hub_part + tile_part.reshape(rows, width)).astype(jnp.bfloat16)
    mixed = jnp.dot(aggregated, weight, preferred_element_type=jnp.float32)
    return jnp.maximum(mixed, 0.0).astype(jnp.bfloat16)[None, None]


def solution(mesh):
    return jax.shard_map(
        per_device,
        mesh=mesh,
        in_specs=(
            P("grp", "blk", None, None),
            P("grp", "blk", None),
            P("grp", "blk", None, None),
            P("grp", "blk", None),
            P("grp", "blk", None),
            P("grp", "blk"),
            P("grp", "blk", None, None, None),
            P("grp", "blk", None, None, None),
            P(),
        ),
        out_specs=P("grp", "blk", None, None),
        check_vma=False,
    )
```

profile of v0, /device:TPU:4, one launch (start us, length us, event | category | flops | bytes accessed | tf_op | source)
XLA Modules:
  0.0 164.9 jit_solution(14965506577353493030)
XLA Ops:
  0.0 0.0 copy-start
  0.0 1.0 reshape_squeeze.3
  1.0 17.8 %gather_fusion.1 = bf16[4096,256]{1,0:T(8,128)(2,1)} fusion(bf16[4096,256]{1,0:T(8,128)(2,1)} %bitcast.45, s32[4096]{0:T(1024)S(1)} %broadcast_clamp_fusion), kind=kCustom, calls=%fused_computation.1 | custom fusion | bytes 4210688 | tf_op jit(solution)/shard_map/gather | solution.py:31
  18.8 0.0 copy-start.4
  18.8 0.0 copy-start.1
  18.8 11.0 %all-to-all-start = ((bf16[128,32,256]{2,1,0:T(8,128)(2,1)}), bf16[128,32,256]{2,1,0:T(8,128)(2,1)}, u32[]{:S(2)}, u32[]{:S(2)}) async-start(bf16[128,32,256]{2,1,0:T(8,128)(2,1)} %bitcast.51), calls=%async_computation | async-start | bytes 4194304 | tf_op jit(solution)/shard_map/all_to_all | solution.py:32
  30.4 0.0 copy-done.4
  30.5 0.0 copy-done.1
  30.5 0.6 gather_fusion
  31.1 42.1 %all-gather = bf16[512,256]{1,0:T(8,128)(2,1)S(1)} all-gather(bf16[32,256]{1,0:T(8,128)(2,1)S(1)} %gather_fusion), channel_id=2, replica_groups=mesh['grp'=8,'blk'=16] {'blk'}, dimensions={0}, use_global_device_ids=true | all-gather | bytes 278528 | tf_op jit(solution)/shard_map/all_gather | solution.py:27
  73.2 0.0 all-to-all-done
  73.2 3.8 %pad_maximum_fusion = bf16[8192,256]{1,0:T(8,128)(2,1)} fusion(bf16[4096,256]{1,0:T(8,128)(2,1)} %bitcast.10, bf16[4096,256]{1,0:T(8,128)(2,1)S(1)} %bitcast.47), kind=kLoop, calls=%fused_computation.11 | loop fusion | flops 8388608 | bytes 8388608 | tf_op jit(solution)/shard_map/concatenate | solution.py:33
  77.0 0.0 copy-start.2
  77.0 7.4 %reshape.76 = bf16[64,32768]{1,0:T(8,128)(2,1)} reshape(bf16[8192,256]{1,0:T(8,128)(2,1)} %pad_maximum_fusion) | data formatting | bytes 8388608 | tf_op jit(solution)/shard_map/reshape | solution.py:35
  84.4 0.0 copy-done.2
  84.4 7.7 %convolution_convert_fusion = bf16[160,32768]{1,0:T(8,128)(2,1)} fusion(bf16[64,32768]{1,0:T(8,128)(2,1)} %reshape.76, s32[160]{0:T(256)S(1)} %bitcast.53), kind=kOutput, calls=%fused_computation.2 | convolution fusion | flops 676341760 | bytes 14680704 | tf_op jit(solution)/shard_map/dot_general | solution.py:40
  92.1 11.2 %copy.14 = bf16[20,8,128,256]{3,2,1,0:T(8,128)(2,1)} copy(bf16[20,8,128,256]{3,1,2,0:T(8,128)(2,1)} %bitcast.50) | data formatting | bytes 20971520
  103.4 15.6 %convolution_bitcast_fusion = f32[160,128,256]{1,2,0:T(8,128)} fusion(bf16[160,128,256]{2,1,0:T(8,128)(2,1)} %bitcast.48, bf16[1,1,160,128,128]{4,3,2,1,0:T(8,128)(2,1)} %param.15), kind=kOutput, calls=%fused_computation.3 | convolution fusion | flops 1342177280 | bytes 36700160 | tf_op jit(solution)/shard_map/tij,tjf->tif/dot_general | solution.py:42
  119.0 21.3 %copy.15 = f32[20,8,128,256]{3,1,2,0:T(8,128)} copy(f32[20,8,128,256]{2,3,1,0:T(8,128)} %bitcast.44) | data formatting | bytes 41943040
  140.3 0.0 copy-done.3
  140.3 13.0 %fusion.10 = f32[32,32768]{1,0:T(8,128)} fusion(f32[160,32768]{1,0:T(8,128)} %bitcast.49, s32[160]{0:T(256)S(1)} %bitcast.54, pred[160]{0:T(512)(128)(4,1)S(1)} %iota_compare_fusion.3), kind=kOutput, calls=%fused_computation.18 | convolution fusion | flops 2013276160 | bytes 25166624 | tf_op jit(solution)/shard_map/dot_general | solution.py:51
  153.2 4.9 %reshape.79 = f32[4096,256]{1,0:T(8,128)} reshape(f32[32,32768]{1,0:T(8,128)} %fusion.10) | data formatting | bytes 8388608 | tf_op jit(solution)/shard_map/reshape | solution.py:57
  158.1 0.0 copy-done
  158.1 6.7 %fusion.4 = bf16[1,1,4096,256]{3,2,1,0:T(8,128)(2,1)} fusion(bf16[256,256]{1,0:T(8,128)(2,1)S(1)} %copy-done, f32[4096,256]{1,0:T(8,128)} %reshape.79, bf16[512,256]{1,0:T(8,128)(2,1)S(1)} %all-gather, bf16[1,1,4096,512]{3,2,1,0:T(8,128)(2,1)} %param.11), kind=kOutput, calls=%fused_computation.10 | convolution fusion | flops 1614807040 | bytes 10878976 | tf_op jit(solution)/shard_map/dot_general | solution.py:58
  (6 shorter events, 0.0 us)
Async XLA Ops:
  0.0 158.1 %copy-start = (bf16[256,256]{1,0:T(8,128)(2,1)S(1)}, bf16[256,256]{1,0:T(8,128)(2,1)}, u32[]{:S(2)}) copy-start(bf16[256,256]{1,0:T(8,128)(2,1)} %param.17) | copy-start | bytes 393220
  18.8 11.6 %copy-start.4 = (s32[1,1,32]{2,1,0:T(1,128)S(1)}, s32[1,1,32]{2,1,0:T(1,128)}, u32[]{:S(2)}) copy-start(s32[1,1,32]{2,1,0:T(1,128)} %param.10) | copy-start | bytes 388
  18.8 11.7 %copy-start.1 = (bf16[1,1,4096,256]{3,2,1,0:T(8,128)(2,1)S(1)}, bf16[1,1,4096,256]{3,2,1,0:T(8,128)(2,1)}, u32[]{:S(2)}) copy-start(bf16[1,1,4096,256]{3,2,1,0:T(8,128)(2,1)} %param.9) | copy-start | bytes 6291460
  18.8 54.4 %all-to-all-start = ((bf16[128,32,256]{2,1,0:T(8,128)(2,1)}), bf16[128,32,256]{2,1,0:T(8,128)(2,1)}, u32[]{:S(2)}, u32[]{:S(2)}) async-start(bf16[128,32,256]{2,1,0:T(8,128)(2,1)} %bitcast.51), calls=%async_computation | async-start | bytes 4194304 | tf_op jit(solution)/shard_map/all_to_all | solution.py:32
  77.0 7.4 %copy-start.2 = (s32[1,1,160]{2,1,0:T(1,128)S(1)}, s32[1,1,160]{2,1,0:T(1,128)}, u32[]{:S(2)}) copy-start(s32[1,1,160]{2,1,0:T(1,128)} %param.13) | copy-start | bytes 1924
  119.0 21.3 %copy-start.3 = (s32[1,1,160]{2,1,0:T(1,128)S(1)}, s32[1,1,160]{2,1,0:T(1,128)}, u32[]{:S(2)}) copy-start(s32[1,1,160]{2,1,0:T(1,128)} %param.12) | copy-start | bytes 1924
where the time goes:
time: 166 us; the launch traced here: 165 us
  local copies, waits for them, and re-layouts  64.3 us (39%)
  matrix products  43 us (26%)
  blocking collectives  42.1 us (25%)
  starting transfers between devices  11 us (7%)
  other arithmetic  3.85 us (2%)
    all_gather x1, blocking collectives, per_device(): lax.all_gather(hub_block, 'blk', axis=0, tiled=True)  42.1 us
    unnamed x12, local copies, waits for them, and re-layouts  32.6 us
    gather x1, local copies, waits for them, and re-layouts, per_device(): outgoing = local[listing.reshape(-1)]  17.8 us
    dot_general x1, matrix products, per_device(): jnp.einsum('tij,tjf->tif', tile_values[0, 0], picked, preferred_element_t...  15.6 us
    dot_general x1, matrix products, per_device(): jnp.dot(placing, products.reshape(slots, TB * width), precision=lax.Preci...  13 us
    all_to_all x1, starting transfers between devices, per_device(): lax.all_to_all(outgoing, ('grp', 'blk'), split_axis=0, concat_axis=0, til...  11 us
    dot_general x1, matrix products, per_device(): jnp.dot(selector, flat_table, preferred_element_type=jnp.float32)  7.73 us
    reshape x1, local copies, waits for them, and re-layouts, per_device(): flat_table = table.reshape(table_blocks, TB * width)  7.38 us
  transfers between devices with their start and end apart: 1, of which 0 were waited for; matrix products, arithmetic and copies ran while one was open for 0% of the time, Pallas kernels for 0%

commit v1 on v0

--- a/solution.py
+++ b/solution.py
@@ -24,7 +24,9 @@
     hub_block = local[hub_rows[0, 0]]
     hub_part = jnp.dot(
         adjacency,
-        lax.all_gather(hub_block, "blk", axis=0, tiled=True),
+        jnp.concatenate(
+            lax.all_to_all(jnp.stack([hub_block] * lax.axis_size("blk")), "blk", 0, 0), axis=0
+        ),
         preferred_element_type=jnp.float32,
     )
     listing = send_rows[0, 0]

time: 166 us -> 157 us (0.946)
  the two profiles are of different devices: /device:TPU:4 before, /device:TPU:1 now
where the time goes in v1:
time: 157 us; the launch traced here: 156 us
  local copies, waits for them, and re-layouts  65 us (41%)
  matrix products  42.9 us (27%)
  waiting for transfers between devices  27.8 us (18%)
  starting transfers between devices  15.6 us (10%)
  other arithmetic  3.84 us (2%)
    unnamed x12, local copies, waits for them, and re-layouts  32.6 us
    all_to_all x1, waiting for transfers between devices, per_device(): lax.all_to_all(outgoing, ('grp', 'blk'), split_axis=0, concat_axis=0, til...  27.8 us
    gather x1, local copies, waits for them, and re-layouts, per_device(): outgoing = local[listing.reshape(-1)]  17.8 us
    dot_general x1, matrix products, per_device(): jnp.einsum('tij,tjf->tif', tile_values[0, 0], picked, preferred_element_t...  15.6 us
    dot_general x1, matrix products, per_device(): jnp.dot(placing, products.reshape(slots, TB * width), precision=lax.Preci...  12.9 us
    all_to_all x1, starting transfers between devices, per_device(): lax.all_to_all(outgoing, ('grp', 'blk'), split_axis=0, concat_axis=0, til...  12 us
    dot_general x1, matrix products, per_device(): jnp.dot(selector, flat_table, preferred_element_type=jnp.float32)  7.74 us
    reshape x1, local copies, waits for them, and re-layouts, per_device(): flat_table = table.reshape(table_blocks, TB * width)  7.38 us
  transfers between devices with their start and end apart: 2, of which 1 were waited for; matrix products, arithmetic and copies ran while one was open for 55% of the time, Pallas kernels for 0%

profile of v1, /device:TPU:1, one launch (start us, length us, event | category | flops | bytes accessed | tf_op | source)
XLA Modules:
  0.0 155.9 jit_solution(17634149074771361423)
XLA Ops:
  0.0 0.0 copy-start
  0.0 1.0 reshape_squeeze.3
  1.0 17.8 %gather_fusion.1 = bf16[4096,256]{1,0:T(8,128)(2,1)} fusion(bf16[4096,256]{1,0:T(8,128)(2,1)} %bitcast.46, s32[4096]{0:T(1024)S(1)} %broadcast_clamp_fusion), kind=kCustom, calls=%fused_computation.1 | custom fusion | bytes 4210688 | tf_op jit(solution)/shard_map/gather | solution.py:33
  18.8 0.0 copy-start.4
  18.8 12.0 %all-to-all-start.1 = ((bf16[128,32,256]{2,1,0:T(8,128)(2,1)}), bf16[128,32,256]{2,1,0:T(8,128)(2,1)}, u32[]{:S(2)}, u32[]{:S(2)}) async-start(bf16[128,32,256]{2,1,0:T(8,128)(2,1)} %bitcast.52), calls=%async_computation.1 | async-start | bytes 4194304 | tf_op jit(solution)/shard_map/all_to_all | solution.py:34
  31.4 0.0 copy-done.4
  31.5 0.0 copy-done.1
  31.5 0.6 gather_fusion
  32.1 27.8 %all-to-all-done.1 = bf16[128,32,256]{2,1,0:T(8,128)(2,1)} async-done(((bf16[128,32,256]{2,1,0:T(8,128)(2,1)}), bf16[128,32,256]{2,1,0:T(8,128)(2,1)}, u32[]{:S(2)}, u32[]{:S(2)}) %all-to-all-start.1) | async-done | bytes 2097184 | tf_op jit(solution)/shard_map/all_to_all | solution.py:34
  59.9 0.7 stack.2
  60.7 3.7 %all-to-all-start = ((bf16[16,32,256]{2,1,0:T(8,128)(2,1)}), bf16[16,32,256]{2,1,0:T(8,128)(2,1)S(1)}, u32[]{:S(2)}, u32[]{:S(2)}) async-start(bf16[16,32,256]{2,1,0:T(8,128)(2,1)} %stack.2), calls=%async_computation | async-start | bytes 524288 | tf_op jit(solution)/shard_map/all_to_all | solution.py:28
  64.3 3.8 %pad_maximum_fusion = bf16[8192,256]{1,0:T(8,128)(2,1)} fusion(bf16[4096,256]{1,0:T(8,128)(2,1)} %bitcast.11, bf16[4096,256]{1,0:T(8,128)(2,1)S(1)} %bitcast.48), kind=kLoop, calls=%fused_computation.11 | loop fusion | flops 8388608 | bytes 8388608 | tf_op jit(solution)/shard_map/concatenate | solution.py:35
  68.1 7.4 %reshape.82 = bf16[64,32768]{1,0:T(8,128)(2,1)} reshape(bf16[8192,256]{1,0:T(8,128)(2,1)} %pad_maximum_fusion) | data formatting | bytes 8388608 | tf_op jit(solution)/shard_map/reshape | solution.py:37
  75.5 0.0 copy-done.2
  75.5 7.7 %convolution_convert_fusion = bf16[160,32768]{1,0:T(8,128)(2,1)} fusion(bf16[64,32768]{1,0:T(8,128)(2,1)} %reshape.82, s32[160]{0:T(256)S(1)} %bitcast.55), kind=kOutput, calls=%fused_computation.2 | convolution fusion | flops 676341760 | bytes 14680704 | tf_op jit(solution)/shard_map/dot_general | solution.py:42
  83.3 11.2 %copy.14 = bf16[20,8,128,256]{3,2,1,0:T(8,128)(2,1)} copy(bf16[20,8,128,256]{3,1,2,0:T(8,128)(2,1)} %bitcast.51) | data formatting | bytes 20971520
  94.5 15.6 %convolution_bitcast_fusion = f32[160,128,256]{1,2,0:T(8,128)} fusion(bf16[160,128,256]{2,1,0:T(8,128)(2,1)} %bitcast.49, bf16[1,1,160,128,128]{4,3,2,1,0:T(8,128)(2,1)} %param.15), kind=kOutput, calls=%fused_computation.3 | convolution fusion | flops 1342177280 | bytes 36700160 | tf_op jit(solution)/shard_map/tij,tjf->tif/dot_general | solution.py:44
  110.1 21.3 %copy.15 = f32[20,8,128,256]{3,1,2,0:T(8,128)} copy(f32[20,8,128,256]{2,3,1,0:T(8,128)} %bitcast.45) | data formatting | bytes 41943040
  131.4 0.0 copy-done.3
  131.4 12.9 %fusion.10 = f32[32,32768]{1,0:T(8,128)} fusion(f32[160,32768]{1,0:T(8,128)} %bitcast.50, s32[160]{0:T(256)S(1)} %bitcast.56, pred[160]{0:T(512)(128)(4,1)S(1)} %iota_compare_fusion.3), kind=kOutput, calls=%fused_computation.18 | convolution fusion | flops 2013276160 | bytes 25166624 | tf_op jit(solution)/shard_map/dot_general | solution.py:53
  144.3 4.9 %reshape.85 = f32[4096,256]{1,0:T(8,128)} reshape(f32[32,32768]{1,0:T(8,128)} %fusion.10) | data formatting | bytes 8388608 | tf_op jit(solution)/shard_map/reshape | solution.py:59
  149.2 0.0 all-to-all-done
  149.2 0.0 copy-done
  149.2 6.7 %fusion.4 = bf16[1,1,4096,256]{3,2,1,0:T(8,128)(2,1)} fusion(bf16[256,256]{1,0:T(8,128)(2,1)S(1)} %copy-done, f32[4096,256]{1,0:T(8,128)} %reshape.85, bf16[512,256]{1,0:T(8,128)(2,1)S(1)} %bitcast.53, bf16[1,1,4096,512]{3,2,1,0:T(8,128)(2,1)} %param.11), kind=kOutput, calls=%fused_computation.10 | convolution fusion | flops 1614807040 | bytes 10878976 | tf_op jit(solution)/shard_map/dot_general | solution.py:60
  (8 shorter events, 0.0 us)
Async XLA Ops:
  0.0 149.2 %copy-start = (bf16[256,256]{1,0:T(8,128)(2,1)S(1)}, bf16[256,256]{1,0:T(8,128)(2,1)}, u32[]{:S(2)}) copy-start(bf16[256,256]{1,0:T(8,128)(2,1)} %param.17) | copy-start | bytes 393220
  18.8 12.6 %copy-start.4 = (s32[1,1,32]{2,1,0:T(1,128)S(1)}, s32[1,1,32]{2,1,0:T(1,128)}, u32[]{:S(2)}) copy-start(s32[1,1,32]{2,1,0:T(1,128)} %param.10) | copy-start | bytes 388
  18.8 12.7 %copy-start.1 = (bf16[1,1,4096,256]{3,2,1,0:T(8,128)(2,1)S(1)}, bf16[1,1,4096,256]{3,2,1,0:T(8,128)(2,1)}, u32[]{:S(2)}) copy-start(bf16[1,1,4096,256]{3,2,1,0:T(8,128)(2,1)} %param.9) | copy-start | bytes 6291460
  18.8 41.1 %all-to-all-start.1 = ((bf16[128,32,256]{2,1,0:T(8,128)(2,1)}), bf16[128,32,256]{2,1,0:T(8,128)(2,1)}, u32[]{:S(2)}, u32[]{:S(2)}) async-start(bf16[128,32,256]{2,1,0:T(8,128)(2,1)} %bitcast.52), calls=%async_computation.1 | async-start | bytes 4194304 | tf_op jit(solution)/shard_map/all_to_all | solution.py:34
  60.7 88.6 %all-to-all-start = ((bf16[16,32,256]{2,1,0:T(8,128)(2,1)}), bf16[16,32,256]{2,1,0:T(8,128)(2,1)S(1)}, u32[]{:S(2)}, u32[]{:S(2)}) async-start(bf16[16,32,256]{2,1,0:T(8,128)(2,1)} %stack.2), calls=%async_computation | async-start | bytes 524288 | tf_op jit(solution)/shard_map/all_to_all | solution.py:28
  68.1 7.4 %copy-start.2 = (s32[1,1,160]{2,1,0:T(1,128)S(1)}, s32[1,1,160]{2,1,0:T(1,128)}, u32[]{:S(2)}) copy-start(s32[1,1,160]{2,1,0:T(1,128)} %param.13) | copy-start | bytes 1924
  110.1 21.3 %copy-start.3 = (s32[1,1,160]{2,1,0:T(1,128)S(1)}, s32[1,1,160]{2,1,0:T(1,128)}, u32[]{:S(2)}) copy-start(s32[1,1,160]{2,1,0:T(1,128)} %param.12) | copy-start | bytes 1924
